TPU v7x, 512 devices: a whole 4x8x8 slice. The times are simulated.
512 devices in a mesh: freq: 8 (over x, core), geo: 64 (over z, y).
Axes of the slice: x: 4, y: 8, z: 8, core: 2. Of those that a mesh axis runs over, the one named last changes fastest.
Arguments:
- energy: float32 [256, 48, 36, 128], P('geo', 'freq'), may hold values from 0.1 to 1.5
- water_depth: float32 [256, 128], P('geo'), may hold values from 0.5 to 4
- wet_mask: int32 [256, 128], P('geo'), may hold values 0 or 1
- vegetation: int32 [256, 128], P('geo'), may hold values 0 or 1
- canopy: float32 [256, 128], P('geo'), may hold values from 0.004 to 0.04
- quad_offsets: int32 [4], replicated, may hold values from 1 to 3, as said below
- quad_weights: float32 [2], replicated, may hold values from 0.2 to 0.8
Outputs:
- energy_next: float32 [256, 48, 36, 128], P('geo', 'freq')
- orbital: float32 [256, 128], P('geo')
Inputs may be any that keep to these rules, and one draw needn't show every extreme that they name: `quad_offsets`: offsets a and the two direction turns lie in 1 .. 3; the lower frequency offset b equals 3 in every draw.
All inputs are finite; a program needn't handle non-finite values. No bound on the sum of `wet_mask` or of `vegetation` on one device may be relied on, other than what follows from the above.
Results may differ from a plain program's by a relative error of at most 0.00002.
Values sent between devices are 32-bit elements; how exact they have to be, the bound alone decides.
No kernel may reach another device: no remote copies, remote signals or barrier semaphores. Data moves between devices by JAX's collectives and lax.ppermute only.
A program may use at most 64 MiB of HBM per device.

v0:
```python
import math
import jax
import jax.numpy as jnp
from jax import lax
from jax.sharding import PartitionSpec as P

FH = 4
SUBSTEPS = 8
gravity = 9.81
base_freq = 0.03
freq_ratio = 1.05
cell_size = 20.0
sub_step = 2.0
coupling = 0.01
coef_plus = 0.4096
coef_minus = 3.1605
coef_both = 2.589


def from_neighbour(block, axis, distance, cyclic=False):
    count = lax.axis_size(axis)
    if cyclic:
        pairs = [(i, (i + distance) % count) for i in range(count)]
    else:
        pairs = [(i, i + distance) for i in range(count) if 0 <= i + distance < count]
    return lax.ppermute(block, axis, pairs)


def halo(block, axis, dim, width, side, cyclic=False):
    size = block.shape[dim]
    parts = []
    distance = 1
    need = width
    while need > 0:
        take = min(size, need)
        if side < 0:
            piece = lax.slice_in_dim(block, size - take, size, axis=dim)
            parts.insert(0, from_neighbour(piece, axis, distance, cyclic))
        else:
            piece = lax.slice_in_dim(block, 0, take, axis=dim)
            parts.append(from_neighbour(piece, axis, -distance, cyclic))
        need -= take
        distance += 1
    return parts


def butterfly_sum(value, axis):
    count = lax.axis_size(axis)
    assert count & count - 1 == 0
    step = 1
    while step < count:
        value = value + lax.ppermute(value, axis, [(i, i ^ step) for i in range(count)])
        step *= 2
    return value


def gathered_sum(known, index, count, value):
    reach = max(known)
    if count > 2 * (2 * reach + 1) - 2 or count % 2:
        return butterfly_sum(value, "freq")
    far = count // 2
    ordered = jnp.stack([known[o] for o in range(-reach, reach + 1)])
    more = from_neighbour(ordered, "freq", far, True)
    table = []
    for rel in range(count):
        off = rel if rel <= reach else rel - count
        if -reach <= off <= reach:
            table.append(known[off])
        else:
            table.append(more[rel - far + reach])
    table = jnp.stack(table)
    table = jnp.concatenate([table, table], axis=0)
    start = (count - index) % count
    glob = lax.dynamic_slice_in_dim(table, start, count, axis=0)
    while glob.shape[0] > 1:
        glob = glob[0::2] + glob[1::2]
    return glob[0]


def physics(radian_freq, water_depth, dir_count):
    square = (radian_freq * radian_freq)[None, :, None]
    column = water_depth[:, None, :]
    depth_ratio = square * column / gravity
    depth_wave = depth_ratio / jnp.sqrt(jnp.tanh(depth_ratio))
    group_speed = (
        radian_freq[None, :, None]
        * column
        / depth_wave
        * (0.5 + depth_wave / jnp.sinh(2.0 * depth_wave))
    )
    orbit_weight = (
        square
        / jnp.sinh(depth_wave) ** 2
        * (radian_freq * (freq_ratio - 1.0))[None, :, None]
        * (2.0 * math.pi / dir_count)
    )
    return (group_speed, orbit_weight)


def angles_of(dir_count):
    angles = (jnp.arange(dir_count, dtype=jnp.float32) + 0.5) * (2.0 * math.pi / dir_count)
    return (jnp.cos(angles), jnp.sin(angles))


def shifted(doubled, freq_start, dir_off, count):
    dir_count = doubled.shape[2] // 2
    starts = (jnp.zeros((), jnp.int32), freq_start, dir_off % dir_count, jnp.zeros((), jnp.int32))
    return lax.dynamic_slice(
        doubled, starts, (doubled.shape[0], count, dir_count, doubled.shape[3])
    )


def source_change(extended, quad_offsets, quad_weights, count):
    up_bins, down_bins, up_turn, down_turn = (
        quad_offsets[0],
        quad_offsets[1],
        quad_offsets[2],
        quad_offsets[3],
    )
    weight_up, weight_down = (quad_weights[0], quad_weights[1])
    wide = count + 2 * FH
    doubled = jnp.concatenate([extended, extended], axis=2)
    centre = lax.slice_in_dim(extended, FH, FH + wide, axis=1)
    upper = weight_up * shifted(doubled, FH + up_bins, up_turn, wide) + (1.0 - weight_up) * shifted(
        doubled, FH + up_bins + 1, up_turn, wide
    )
    lower = weight_down * shifted(doubled, FH - down_bins, -down_turn, wide) + (
        1.0 - weight_down
    ) * shifted(doubled, FH - down_bins - 1, -down_turn, wide)
    transfer = coupling * (
        centre * centre * (coef_plus * upper + coef_minus * lower)
        - coef_both * centre * upper * lower
    )
    spread = jnp.concatenate([transfer, transfer], axis=2)
    gained = weight_up * shifted(spread, FH - up_bins, -up_turn, count) + (
        1.0 - weight_up
    ) * shifted(spread, FH - up_bins - 1, -up_turn, count)
    gained = (
        gained
        + weight_down * shifted(spread, FH + down_bins, down_turn, count)
        + (1.0 - weight_down) * shifted(spread, FH + down_bins + 1, down_turn, count)
    )
    own = lax.slice_in_dim(transfer, FH, FH + count, axis=1)
    return gained - 2.0 * own


def east_west(east_flux, cosines):
    zeros = jnp.zeros_like(east_flux[..., :1])
    behind = jnp.concatenate([zeros, east_flux[..., :-1]], axis=-1)
    ahead = jnp.concatenate([east_flux[..., 1:], zeros], axis=-1)
    east_going = (cosines > 0.0)[None, None, :, None]
    return jnp.where(east_going, east_flux - behind, ahead - east_flux)


def propagate(spectrum, speed, wet, cosines, sines, northward):
    step_ratio = sub_step / cell_size
    east_speed = speed[:, :, None, :] * cosines[None, None, :, None]
    north_speed = speed[:, :, None, :] * sines[None, None, :, None]
    rows = spectrum.shape[0]
    for substep in range(SUBSTEPS):
        lo, hi = (substep, rows) if northward else (0, rows - substep)
        east_flux = east_speed[lo:hi] * spectrum
        north_flux = north_speed[lo:hi] * spectrum
        along = north_flux[1:] - north_flux[:-1]
        across = east_west(east_flux, cosines)
        if northward:
            spectrum = wet[lo + 1 : hi, None, None, :] * (
                spectrum[1:] - step_ratio * (across[1:] + along)
            )
        else:
            spectrum = wet[lo : hi - 1, None, None, :] * (
                spectrum[:-1] - step_ratio * (across[:-1] + along)
            )
    return spectrum


def body(energy, water_depth, wet_mask, vegetation, canopy, quad_offsets, quad_weights):
    tile_rows, freq_count, dir_count, tile_cols = energy.shape
    wet_field = wet_mask.astype(jnp.float32)
    veg_field = vegetation.astype(jnp.float32)
    wet_four = wet_field[:, None, None, :]
    masked = wet_four * energy
    first_bin = lax.axis_index("freq") * freq_count
    bin_index = (first_bin + jnp.arange(freq_count, dtype=jnp.int32)).astype(jnp.float32)
    radian_freq = 2.0 * math.pi * base_freq * jnp.power(freq_ratio, bin_index)
    half = dir_count // 2
    cosines, sines = angles_of(dir_count)
    fields = jnp.zeros((tile_rows, 1, half, tile_cols), jnp.float32)
    fields = fields.at[:, 0, 0, :].set(wet_field).at[:, 0, 1, :].set(water_depth)
    north_msg = jnp.concatenate([masked[:, :, :half], fields], axis=1)
    south_msg = jnp.concatenate([masked[:, :, half:], fields], axis=1)
    below = halo(north_msg, "geo", 0, SUBSTEPS, -1)
    above = halo(south_msg, "geo", 0, SUBSTEPS, +1)
    group_speed, orbit_weight = physics(radian_freq, water_depth, dir_count)
    partial_value = jnp.sum(orbit_weight * jnp.sum(energy, axis=2), axis=1)
    freq_index = lax.axis_index("freq")
    freq_total = lax.axis_size("freq")
    slot = jnp.zeros((tile_rows, 1, dir_count, tile_cols), jnp.float32)
    slot = slot.at[:, 0, 0, :].set(partial_value)
    gathered = lax.all_gather(jnp.concatenate([masked, slot], axis=1), "freq", axis=1, tiled=True)
    gathered = gathered.reshape(tile_rows, freq_total, freq_count + 1, dir_count, tile_cols)
    partials = gathered[:, :, freq_count, 0, :]
    spectrum_all = gathered[:, :, :freq_count].reshape(
        tile_rows, freq_total * freq_count, dir_count, tile_cols
    )
    padded_all = jnp.pad(spectrum_all, ((0, 0), (2 * FH, 2 * FH), (0, 0), (0, 0)))
    extended = lax.dynamic_slice_in_dim(padded_all, first_bin, freq_count + 4 * FH, axis=1)
    glob = jnp.moveaxis(partials, 1, 0)
    while glob.shape[0] > 1:
        glob = glob[0::2] + glob[1::2]
    orbital = jnp.sqrt(glob[0])
    full_step = SUBSTEPS * sub_step
    damping = 1.0 + full_step * canopy * veg_field * orbital
    change = source_change(extended, quad_offsets, quad_weights, freq_count)
    increment = (masked + full_step * change) / damping[:, None, None, :] - masked
    geo_index = lax.axis_index("geo")
    geo_count = lax.axis_size("geo")

    def unpack(parts, offsets):
        spectra, speeds, wets = ([], [], [])
        for part, offset in zip(parts, offsets):
            valid = (geo_index + offset >= 0) & (geo_index + offset < geo_count)
            depth = jnp.where(valid, part[:, freq_count, 1, :], 1.0)
            spectra.append(part[:, :freq_count])
            wets.append(part[:, freq_count, 0, :])
            speeds.append(physics(radian_freq, depth, dir_count)[0])
        return (spectra, speeds, wets)

    n_off = [-(len(below) - k) for k in range(len(below))]
    b_spec, b_speed, b_wet = unpack(below, n_off)
    north = propagate(
        jnp.concatenate(b_spec + [masked[:, :, :half]], axis=0),
        jnp.concatenate(b_speed + [group_speed], axis=0),
        jnp.concatenate(b_wet + [wet_field], axis=0),
        cosines[:half],
        sines[:half],
        True,
    )
    s_off = [k + 1 for k in range(len(above))]
    a_spec, a_speed, a_wet = unpack(above, s_off)
    south = propagate(
        jnp.concatenate([masked[:, :, half:]] + a_spec, axis=0),
        jnp.concatenate([group_speed] + a_speed, axis=0),
        jnp.concatenate([wet_field] + a_wet, axis=0),
        cosines[half:],
        sines[half:],
        False,
    )
    moved = jnp.concatenate([north, south], axis=2)
    return (wet_four * (moved + increment), orbital)


def solution(mesh):
    placed = (
        P("geo", "freq", None, None),
        P("geo", None),
        P("geo", None),
        P("geo", None),
        P("geo", None),
        P(),
        P(),
    )
    return jax.shard_map(
        body,
        mesh=mesh,
        in_specs=placed,
        out_specs=(P("geo", "freq", None, None), P("geo", None)),
        check_vma=False,
    )
```

profile of v0, /device:TPU:1, one launch (start us, length us, event | category | flops | bytes accessed | tf_op | source)
XLA Modules:
  0.0 115.2 jit_solution(11909362313528127280)
XLA Ops:
  7.2 0.7 fusion.169
  7.9 1.1 fusion.159
  9.1 0.6 slice.640
  9.7 1.3 %constant_dynamic-update-slice_fusion = f32[4,1,18,128]{3,0,2,1:T(4,128)S(1)} fusion(f32[4,1,18,128]{3,0,2,1:T(4,128)S(1)} %scatter.10, s32[]{:T(128)} %bitcast.2, f32[4,128]{1,0:T(4,128)} %param.14), kind=kLoop, calls=%fused_computation.258 | loop fusion | bytes 4100 | tf_op jit(solution)/shard_map/scatter | solution.py:189
  11.1 1.3 %collective-permute-start.2 = (f32[4,7,18,128]{3,0,2,1:T(4,128)S(1)}, f32[4,7,18,128]{3,0,2,1:T(4,128)S(1)}, u32[]{:S(2)}, u32[]{:S(2)}) collective-permute-start(f32[4,7,18,128]{3,0,2,1:T(4,128)S(1)} %get-tuple-element.123), channel_id=1, source_target_pairs={{1,0},{2,1},{3,2},{4,3},{5,4},{6,5},{7,6},{8,7},{9,8},{10,9},{11,1... | collective-permute-start | bytes 774152 | tf_op jit(solution)/shard_map/ppermute | solution.py:26
  12.4 1.3 %collective-permute-start.3 = (f32[4,7,18,128]{3,0,2,1:T(4,128)S(1)}, f32[4,7,18,128]{3,0,2,1:T(4,128)S(1)}, u32[]{:S(2)}, u32[]{:S(2)}) collective-permute-start(f32[4,7,18,128]{3,0,2,1:T(4,128)S(1)} %get-tuple-element.123), channel_id=1, source_target_pairs={{2,0},{3,1},{4,2},{5,3},{6,4},{7,5},{8,6},{9,7},{10,8},{11,9},{12,... | collective-permute-start | bytes 774152 | tf_op jit(solution)/shard_map/ppermute | solution.py:26
  13.7 6.5 %collective-permute-start.1 = (f32[4,7,18,128]{3,0,2,1:T(4,128)S(1)}, f32[4,7,18,128]{3,0,2,1:T(4,128)S(1)}, u32[]{:S(2)}, u32[]{:S(2)}) collective-permute-start(f32[4,7,18,128]{3,0,2,1:T(4,128)S(1)} %get-tuple-element.122), channel_id=1, source_target_pairs={{0,2},{1,3},{2,4},{3,5},{4,6},{5,7},{6,8},{7,9},{8,10},{9,11},{10,... | collective-permute-start | bytes 774152 | tf_op jit(solution)/shard_map/ppermute | solution.py:26
  20.2 3.2 %collective-permute-start = (f32[4,7,18,128]{3,0,2,1:T(4,128)S(1)}, f32[4,7,18,128]{3,0,2,1:T(4,128)S(1)}, u32[]{:S(2)}, u32[]{:S(2)}) collective-permute-start(f32[4,7,18,128]{3,0,2,1:T(4,128)S(1)} %get-tuple-element.122), channel_id=1, source_target_pairs={{0,1},{1,2},{2,3},{3,4},{4,5},{5,6},{6,7},{7,8},{8,9},{9,10},{10,1... | collective-permute-start | bytes 774152 | tf_op jit(solution)/shard_map/ppermute | solution.py:26
  23.6 0.5 fusion.172
  24.1 1.3 %fusion.170 = (f32[1]{0:T(128)}, f32[1]{0:T(128)}) fusion(f32[2]{0:T(128)} %param.19), kind=kLoop, calls=%fused_computation.307 | loop fusion | bytes 16 | tf_op jit(solution)/shard_map/slice | solution.py:120
  25.4 1.5 %fusion.171 = (s32[1]{0:T(128)}, s32[1]{0:T(128)}, s32[1]{0:T(128)}, s32[1]{0:T(128)}) fusion(s32[4]{0:T(128)} %param.18), kind=kLoop, calls=%fused_computation.308 | loop fusion | bytes 32 | tf_op jit(solution)/shard_map/slice | solution.py:117
  40.5 0.6 slice.815
  41.1 0.6 slice.814
  41.7 0.6 slice.813
  42.3 0.6 slice.644
  42.9 0.6 slice.643
  43.5 0.6 slice.642
  44.1 1.0 multiply_reduce_fusion
  45.1 0.6 pad_maximum_fusion.4
  45.8 0.4 fusion.96
  46.2 0.3 fusion.158
  46.6 0.6 slice_multiply_fusion.5
  47.1 0.3 fusion.157
  47.6 0.6 slice_multiply_fusion.3
  48.1 0.3 fusion.156
  48.6 0.6 slice_multiply_fusion.1
  49.1 0.3 fusion.155
  49.6 0.3 slice_multiply_fusion.20
  49.9 0.2 fusion.168
  50.2 0.3 slice_multiply_fusion.18
  50.5 0.2 fusion.167
  50.8 0.3 slice_multiply_fusion.16
  51.1 0.2 fusion.166
  51.3 0.3 slice_multiply_fusion.14
  51.7 0.2 fusion.165
  51.9 0.9 select_maximum_fusion
  52.8 1.0 slice.817
  53.8 1.2 %fusion.94 = (f32[12,6,18,128]{3,0,2,1:T(8,128)S(1)}, f32[12,6,18,128]{3,0,2,1:T(8,128)S(1)}, f32[12,6,18,128]{3,0,2,1:T(8,128)S(1)}, f32[12,6,18,128]{3,0,2,1:T(8,128)S(1)}, f32[12,6,18,128]{3,0,2,1:T(8,128)S(1)}) fusion(f32[18]{0:T(128)} %get-tuple-element.155, f32[12,6,128]{2,0,1:T(8,128)} %get-tuple-element.124, ...), kind=kLoop, calls=%fused_computation.195 | loop fusion | flops 995328 | bytes 4018320 | tf_op jit(solution)/shard_map/mul | solution.py:162
  55.1 0.3 fusion.154
  55.4 0.8 slice_multiply_fusion.11
  56.2 0.3 fusion.153
  56.5 0.1 slice_multiply_fusion.10
  56.6 0.2 copy-done.4
  56.8 0.8 slice_multiply_fusion.9
  57.6 0.3 fusion.152
  58.1 0.2 copy-done.3
  58.3 0.8 slice_multiply_fusion.7
  59.1 0.3 fusion.151
  59.5 0.5 slice_multiply_fusion.28
  60.0 0.2 fusion.163
  60.3 0.4 slice_multiply_fusion.26
  60.7 0.2 fusion.162
  61.0 0.6 slice_multiply_fusion.24
  61.5 0.2 fusion.161
  61.8 0.4 slice_multiply_fusion.22
  62.2 0.2 fusion.160
  62.5 0.6 fusion.106
  63.2 34.5 %all-gather.2.cloned.1.call-done = f32[4,56,36,128]{3,0,2,1:T(4,128)} async-done(((f32[4,7,36,128]{3,0,2,1:T(4,128)}), f32[4,56,36,128]{3,0,2,1:T(4,128)}) %all-gather.2.cloned.1.call-update) | async-done | bytes 4128784 | tf_op jit(solution)/shard_map/all_gather | solution.py:200
  97.6 2.2 %slice.954 = f32[4,8,6,36,128]{4,0,3,2,1:T(4,128)S(1)} slice(f32[4,8,7,36,128]{4,0,3,2,1:T(4,128)} %bitcast.61), slice={[0:4], [0:8], [0:6], [0:36], [0:128]} | slice | bytes 7077888 | tf_op jit(solution)/shard_map/slice | solution.py:203
  99.9 0.7 slice_bitcast_fusion
  100.6 0.3 pad_dynamic-slice_fusion.1
  101.0 0.6 multiply_add_fusion
  101.6 3.8 %subtract_multiply_fusion = f32[4,14,36,128]{3,0,2,1:T(4,128)S(1)} fusion(s32[]{:T(128)S(6)} %select_n.216, s32[]{:T(128)S(6)} %select_n.215, f32[4,22,36,128]{3,0,2,1:T(4,128)S(1)} %pad_dynamic-slice_fusion.1, s32[]{:T(128)S(6)} %select_n.213, s32[]{:T(128)S(6)} %select_n.212, s32[]{:T(128)S(6)} %select_n.211, s32[]{:T(128)S(6)} %select_n.209, ...), kind=kLoop, calls=%fused_computation.28 | loop fusion | flops 5160960 | bytes 6193196 | tf_op jit(solution)/shard_map/mul | solution.py:130
  105.4 3.0 %fusion.93 = f32[4,6,36,128]{3,0,2,1:T(4,128)} fusion(f32[4,6,18,128]{3,0,2,1:T(4,128)S(1)} %get-tuple-element.129, f32[4,6,18,128]{3,0,2,1:T(4,128)S(1)} %get-tuple-element.128, f32[4,14,36,128]{3,0,2,1:T(4,128)S(1)} %subtract_multiply_fusion, s32[]{:T(128)S(6)} %select_n.224, s32[]{:T(128)S(6)} %select_n.223, s32[]{:T(128)S(6)} %select_n.221, ...), kind=kLoop, calls=%fused_computation.192 | loop fusion | flops 2322432 | bytes 2805800 | tf_op jit(solution)/shard_map/mul | solution.py:250
  (60 shorter events, 1.8 us)
Async XLA Ops:
  7.2 90.5 %all-gather.2.cloned.1.call-start = ((), (), s32[]{:S(2)}) async-start(), calls=%async_computation | async-start | bytes 4644864 | tf_op jit(solution)/shard_map/all_gather | solution.py:200
  11.1 29.2 %collective-permute-start.2 = (f32[4,7,18,128]{3,0,2,1:T(4,128)S(1)}, f32[4,7,18,128]{3,0,2,1:T(4,128)S(1)}, u32[]{:S(2)}, u32[]{:S(2)}) collective-permute-start(f32[4,7,18,128]{3,0,2,1:T(4,128)S(1)} %get-tuple-element.123), channel_id=1, source_target_pairs={{1,0},{2,1},{3,2},{4,3},{5,4},{6,5},{7,6},{8,7},{9,8},{10,9},{11,1... | collective-permute-start | bytes 774152 | tf_op jit(solution)/shard_map/ppermute | solution.py:26
  12.4 28.0 %collective-permute-start.3 = (f32[4,7,18,128]{3,0,2,1:T(4,128)S(1)}, f32[4,7,18,128]{3,0,2,1:T(4,128)S(1)}, u32[]{:S(2)}, u32[]{:S(2)}) collective-permute-start(f32[4,7,18,128]{3,0,2,1:T(4,128)S(1)} %get-tuple-element.123), channel_id=1, source_target_pairs={{2,0},{3,1},{4,2},{5,3},{6,4},{7,5},{8,6},{9,7},{10,8},{11,9},{12,... | collective-permute-start | bytes 774152 | tf_op jit(solution)/shard_map/ppermute | solution.py:26
  13.7 26.7 %collective-permute-start.1 = (f32[4,7,18,128]{3,0,2,1:T(4,128)S(1)}, f32[4,7,18,128]{3,0,2,1:T(4,128)S(1)}, u32[]{:S(2)}, u32[]{:S(2)}) collective-permute-start(f32[4,7,18,128]{3,0,2,1:T(4,128)S(1)} %get-tuple-element.122), channel_id=1, source_target_pairs={{0,2},{1,3},{2,4},{3,5},{4,6},{5,7},{6,8},{7,9},{8,10},{9,11},{10,... | collective-permute-start | bytes 774152 | tf_op jit(solution)/shard_map/ppermute | solution.py:26
  20.2 20.2 %collective-permute-start = (f32[4,7,18,128]{3,0,2,1:T(4,128)S(1)}, f32[4,7,18,128]{3,0,2,1:T(4,128)S(1)}, u32[]{:S(2)}, u32[]{:S(2)}) collective-permute-start(f32[4,7,18,128]{3,0,2,1:T(4,128)S(1)} %get-tuple-element.122), channel_id=1, source_target_pairs={{0,1},{1,2},{2,3},{3,4},{4,5},{5,6},{6,7},{7,8},{8,9},{9,10},{10,1... | collective-permute-start | bytes 774152 | tf_op jit(solution)/shard_map/ppermute | solution.py:26
  40.4 5.4 %copy-start.2 = (f32[4,7,18,128]{3,0,2,1:T(4,128)}, f32[4,7,18,128]{3,0,2,1:T(4,128)S(1)}, u32[]{:S(2)}) copy-start(f32[4,7,18,128]{3,0,2,1:T(4,128)S(1)} %collective-permute-done) | copy-start | bytes 774148
  40.4 6.1 %copy-start.1 = (f32[4,7,18,128]{3,0,2,1:T(4,128)}, f32[4,7,18,128]{3,0,2,1:T(4,128)S(1)}, u32[]{:S(2)}) copy-start(f32[4,7,18,128]{3,0,2,1:T(4,128)S(1)} %collective-permute-done.1) | copy-start | bytes 774148
  51.7 2.1 %slice-start = ((f32[4,7,18,128]{3,0,2,1:T(4,128)}), f32[4,6,18,128]{3,0,2,1:T(4,128)S(1)}, s32[]{:S(2)}) async-start(f32[4,7,18,128]{3,0,2,1:T(4,128)} %copy-done.1), calls=%async_computation.1 | async-start | bytes 442368 | tf_op jit(solution)/shard_map/slice | solution.py:224
  53.8 1.6 %copy-start.5 = (f32[11,128]{1,0:T(8,128)S(1)}, f32[11,128]{1,0:T(8,128)}, u32[]{:S(2)}) copy-start(f32[11,128]{1,0:T(8,128)} %slice.815) | copy-start | bytes 16900
  56.1 0.7 copy-start.4
  57.6 0.7 copy-start.3
  59.5 0.8 copy-start.8
  60.3 0.7 copy-start.7
  61.0 0.9 copy-start.6
  99.9 1.1 copy-start.9
  99.9 1.1 copy-start.10
  101.0 4.4 %copy-start = (f32[4,6,36,128]{3,0,2,1:T(4,128)S(1)}, f32[4,6,36,128]{3,0,2,1:T(4,128)}, u32[]{:S(2)}) copy-start(f32[4,6,36,128]{3,0,2,1:T(4,128)} %param.13) | copy-start | bytes 1327108
Sparse Core Ops, SparseCore 0:
  52.9 44.6 all-gather.1
where the time goes:
time: 116 us; the launch traced here: 115 us
  waiting for transfers between devices  34.5 us (30%)
  between operations  28 us (24%)
  other arithmetic  22.8 us (20%)
  local copies, waits for them, and re-layouts  17.7 us (15%)
  starting transfers between devices  12.3 us (11%)
    all_gather x1, waiting for transfers between devices, body(): lax.all_gather(jnp.concatenate([masked, slot], axis=1), 'freq', axis=1, t...  34.5 us
    ppermute x4, starting transfers between devices, from_neighbour(): return lax.ppermute(block, axis, pairs)  12.3 us
    mul x16, other arithmetic, propagate(): east_flux = east_speed[lo:hi] * spectrum  8.76 us
    slice x16, local copies, waits for them, and re-layouts, east_west(): behind = jnp.concatenate([zeros, east_flux[..., :-1]], axis=-1)  3.96 us
    mul x1, other arithmetic, source_change(): coupling * (centre * centre * (coef_plus * upper + coef_minus * lower) -...  3.76 us
    slice x6, local copies, waits for them, and re-layouts, propagate(): wet[lo + 1:hi, None, None, :]  3.61 us
    mul x1, other arithmetic, body(): return (wet_four * (moved + increment), orbital)  3.01 us
  transfers between devices with their start and end apart: 5, of which 1 were waited for; matrix products, arithmetic and copies ran while one was open for 11% of the time, Pallas kernels for 0%

commit v1 on v0

--- a/solution.py
+++ b/solution.py
@@ -197,7 +197,11 @@
     freq_total = lax.axis_size("freq")
     slot = jnp.zeros((tile_rows, 1, dir_count, tile_cols), jnp.float32)
     slot = slot.at[:, 0, 0, :].set(partial_value)
-    gathered = lax.all_gather(jnp.concatenate([masked, slot], axis=1), "freq", axis=1, tiled=True)
+    part_2 = jnp.concatenate([masked, slot], axis=1)
+    count_2 = lax.axis_size("freq")
+    pieces = jnp.stack([part_2 for _ in range(count_2)])
+    pieces = lax.all_to_all(pieces, "freq", split_axis=0, concat_axis=0)
+    gathered = jnp.concatenate(pieces, axis=1)
     gathered = gathered.reshape(tile_rows, freq_total, freq_count + 1, dir_count, tile_cols)
     partials = gathered[:, :, freq_count, 0, :]
     spectrum_all = gathered[:, :, :freq_count].reshape(

time: 116 us -> 124 us (1.069)
  between operations: 28 us -> 15.2 us
  starting transfers between devices: 12.3 us -> 23.9 us
  waiting for transfers between devices: 34.5 us -> 41 us
  other arithmetic: 22.8 us -> 25.2 us
    all_to_all x0 -> x1, waiting for transfers between devices: none -> 41 us  [body(): pieces = lax.all_to_all(pieces, 'freq', split_axis=0, concat_axis=0)]
    all_gather x1 -> x0, waiting for transfers between devices: 34.5 us -> none  [body(): lax.all_gather(jnp.concatenate([masked, slot], axis=1), 'freq', axis=1, t...]
    all_to_all x0 -> x1, starting transfers between devices: none -> 11.6 us  [body(): pieces = lax.all_to_all(pieces, 'freq', split_axis=0, concat_axis=0)]
    slice x6, local copies, waits for them, and re-layouts: 3.61 us -> 0.03 us  [propagate(): wet[lo + 1:hi, None, None, :]]
    another operation x2 -> x3, local copies, waits for them, and re-layouts: 0.58 us -> 3.11 us  [the longest x1 2.53 us: body(): pieces = jnp.stack([part_2 for _ in range(count_2)])]
    slice x16, local copies, waits for them, and re-layouts: 3.96 us -> 6.08 us  [east_west(): behind = jnp.concatenate([zeros, east_flux[..., :-1]], axis=-1)]
    mul x14, other arithmetic: 1.34 us -> 3.3 us  [propagate(): north_flux = north_speed[lo:hi] * spectrum]
    mul x16, other arithmetic: 8.76 us -> 10.4 us  [propagate(): east_flux = east_speed[lo:hi] * spectrum]
  transfers between devices with their start and end apart: 5 -> 5, of which waited for: 1 -> 1; matrix products, arithmetic and copies ran while one was open for 11% -> 8% of each run, Pallas kernels for 0% -> 0%
where the time goes in v1:
time: 124 us
  waiting for transfers between devices  41 us (33%)
  other arithmetic  25.2 us (20%)
  starting transfers between devices  23.9 us (19%)
  local copies, waits for them, and re-layouts  18.3 us (15%)
  between operations  15.2 us (12%)
    all_to_all x1, waiting for transfers between devices, body(): pieces = lax.all_to_all(pieces, 'freq', split_axis=0, concat_axis=0)  41 us
    ppermute x4, starting transfers between devices, from_neighbour(): return lax.ppermute(block, axis, pairs)  12.3 us
    all_to_all x1, starting transfers between devices, body(): pieces = lax.all_to_all(pieces, 'freq', split_axis=0, concat_axis=0)  11.6 us
    mul x16, other arithmetic, propagate(): east_flux = east_speed[lo:hi] * spectrum  10.4 us
    slice x16, local copies, waits for them, and re-layouts, east_west(): behind = jnp.concatenate([zeros, east_flux[..., :-1]], axis=-1)  6.08 us
    mul x1, other arithmetic, source_change(): coupling * (centre * centre * (coef_plus * upper + coef_minus * lower) -...  3.88 us
    mul x14, other arithmetic, propagate(): north_flux = north_speed[lo:hi] * spectrum  3.3 us
    mul x1, other arithmetic, body(): return (wet_four * (moved + increment), orbital)  3.13 us
  transfers between devices with their start and end apart: 5, of which 1 were waited for; matrix products, arithmetic and copies ran while one was open for 8% of the time, Pallas kernels for 0%

profile of v1, /device:TPU:1, one launch (start us, length us, event | category | flops | bytes accessed | tf_op | source)
XLA Modules:
  0.0 123.6 jit_solution(9223742887352788762)
XLA Ops:
  0.6 0.7 fusion.169
  1.3 1.1 fusion.159
  2.4 0.8 copy-done.3
  3.2 0.6 slice.640
  3.8 1.3 %constant_dynamic-update-slice_fusion = f32[4,1,18,128]{3,0,2,1:T(4,128)S(1)} fusion(f32[4,1,18,128]{3,0,2,1:T(4,128)S(1)} %scatter.10, s32[]{:T(128)} %bitcast.2, f32[4,128]{1,0:T(4,128)} %param.14), kind=kLoop, calls=%fused_computation.258 | loop fusion | bytes 4100 | tf_op jit(solution)/shard_map/scatter | solution.py:189
  5.2 0.1 pad_maximum_fusion.3
  5.3 1.3 %collective-permute-start.2 = (f32[4,7,18,128]{3,0,2,1:T(4,128)S(1)}, f32[4,7,18,128]{3,0,2,1:T(4,128)S(1)}, u32[]{:S(2)}, u32[]{:S(2)}) collective-permute-start(f32[4,7,18,128]{3,0,2,1:T(4,128)S(1)} %get-tuple-element.123), channel_id=1, source_target_pairs={{1,0},{2,1},{3,2},{4,3},{5,4},{6,5},{7,6},{8,7},{9,8},{10,9},{11,1... | collective-permute-start | bytes 774152 | tf_op jit(solution)/shard_map/ppermute | solution.py:26
  6.6 1.3 %collective-permute-start.3 = (f32[4,7,18,128]{3,0,2,1:T(4,128)S(1)}, f32[4,7,18,128]{3,0,2,1:T(4,128)S(1)}, u32[]{:S(2)}, u32[]{:S(2)}) collective-permute-start(f32[4,7,18,128]{3,0,2,1:T(4,128)S(1)} %get-tuple-element.123), channel_id=1, source_target_pairs={{2,0},{3,1},{4,2},{5,3},{6,4},{7,5},{8,6},{9,7},{10,8},{11,9},{12,... | collective-permute-start | bytes 774152 | tf_op jit(solution)/shard_map/ppermute | solution.py:26
  7.9 6.5 %collective-permute-start.1 = (f32[4,7,18,128]{3,0,2,1:T(4,128)S(1)}, f32[4,7,18,128]{3,0,2,1:T(4,128)S(1)}, u32[]{:S(2)}, u32[]{:S(2)}) collective-permute-start(f32[4,7,18,128]{3,0,2,1:T(4,128)S(1)} %get-tuple-element.122), channel_id=1, source_target_pairs={{0,2},{1,3},{2,4},{3,5},{4,6},{5,7},{6,8},{7,9},{8,10},{9,11},{10,... | collective-permute-start | bytes 774152 | tf_op jit(solution)/shard_map/ppermute | solution.py:26
  14.4 3.2 %collective-permute-start = (f32[4,7,18,128]{3,0,2,1:T(4,128)S(1)}, f32[4,7,18,128]{3,0,2,1:T(4,128)S(1)}, u32[]{:S(2)}, u32[]{:S(2)}) collective-permute-start(f32[4,7,18,128]{3,0,2,1:T(4,128)S(1)} %get-tuple-element.122), channel_id=1, source_target_pairs={{0,1},{1,2},{2,3},{3,4},{4,5},{5,6},{6,7},{7,8},{8,9},{9,10},{10,1... | collective-permute-start | bytes 774152 | tf_op jit(solution)/shard_map/ppermute | solution.py:26
  17.9 1.4 %fusion.170 = (f32[1]{0:T(128)}, f32[1]{0:T(128)}) fusion(f32[2]{0:T(128)} %param.19), kind=kLoop, calls=%fused_computation.307 | loop fusion | bytes 16 | tf_op jit(solution)/shard_map/slice | solution.py:120
  19.2 1.4 %fusion.171 = (s32[1]{0:T(128)}, s32[1]{0:T(128)}, s32[1]{0:T(128)}, s32[1]{0:T(128)}) fusion(s32[4]{0:T(128)} %param.18), kind=kLoop, calls=%fused_computation.308 | loop fusion | bytes 32 | tf_op jit(solution)/shard_map/slice | solution.py:117
  34.9 1.0 multiply_reduce_fusion
  35.9 0.4 fusion.96
  36.4 0.3 fusion.158
  36.7 0.6 slice_multiply_fusion.5
  37.2 0.3 fusion.157
  37.6 0.1 slice_multiply_fusion.4
  37.7 0.6 slice_multiply_fusion.3
  38.2 0.3 fusion.156
  38.7 0.6 slice_multiply_fusion.1
  39.2 0.3 fusion.155
  39.7 0.3 slice_multiply_fusion.20
  40.0 0.2 fusion.168
  40.3 0.3 slice_multiply_fusion.18
  40.6 0.2 fusion.167
  40.8 0.3 slice_multiply_fusion.16
  41.1 0.2 fusion.166
  41.4 1.0 slice_multiply_fusion.14
  42.5 1.1 fusion.165
  43.6 0.4 fusion.94
  44.1 0.3 fusion.154
  44.4 0.7 slice_multiply_fusion.11
  45.1 0.3 fusion.153
  45.4 0.1 slice_multiply_fusion.10
  45.5 0.7 slice_multiply_fusion.9
  46.3 0.3 fusion.152
  46.6 0.1 slice_multiply_fusion.8
  46.7 0.7 slice_multiply_fusion.7
  47.5 1.5 %fusion.151 = (f32[9,6,18,127]{3,0,2,1:T(8,128)}, f32[9,6,18,127]{3,0,2,1:T(8,128)}) fusion(f32[9,6,18,128]{3,0,2,1:T(8,128)S(1)} %get-tuple-element.48), kind=kLoop, calls=%fused_computation.288 | loop fusion | bytes 1975104 | tf_op jit(solution)/shard_map/slice | solution.py:149
  49.0 1.1 slice_multiply_fusion.6
  50.2 2.5 %stack.2 = f32[8,4,7,36,128]{4,1,3,2,0:T(4,128)} broadcast(f32[4,7,36,128]{3,0,2,1:T(4,128)S(1)} %select_maximum_fusion), dimensions={1,2,3,4} | broadcast | bytes 4644864 | tf_op jit(solution)/shard_map/stack | solution.py:202
  52.7 11.6 %all-to-all-start = ((f32[8,4,7,36,128]{4,1,3,2,0:T(4,128)}), f32[8,4,7,36,128]{4,1,3,2,0:T(4,128)}, u32[]{:S(2)}, u32[]{:S(2)}) async-start(f32[8,4,7,36,128]{4,1,3,2,0:T(4,128)} %stack.2), calls=%async_computation | async-start | bytes 8257536 | tf_op jit(solution)/shard_map/all_to_all | solution.py:203
  64.3 1.1 slice_multiply_fusion.13
  65.4 2.5 %slice_multiply_fusion.28 = (f32[8,6,18,128]{3,0,2,1:T(8,128)S(1)}, f32[8,6,18,128]{3,0,2,1:T(8,128)S(1)}) fusion(f32[12,6,18,128]{3,0,2,1:T(8,128)S(1)} %get-tuple-element.121, f32[9,6,18,128]{3,0,2,1:T(8,128)} %slice_multiply_fusion.6, f32[9,6,18,127]{3,0,2,1:T(8,128)} %get-tuple-element.69, f32[9,6,18,127]{3,0,2,1:T(8,128)} %get-tuple-element.68, ...), kind=kLoop, calls=%fused_computation.179 | loop fusion | flops 995328 | bytes 4088242 | tf_op jit(solution)/shard_map/mul | solution.py:162
  68.0 0.2 fusion.163
  68.3 0.4 slice_multiply_fusion.26
  68.7 0.2 fusion.162
  68.9 0.4 slice_multiply_fusion.24
  69.3 0.2 fusion.161
  69.7 0.4 slice_multiply_fusion.22
  70.1 0.2 fusion.160
  70.3 0.3 copy-done.2
  70.6 0.1 copy-done.5
  70.8 0.1 copy-done.7
  70.9 0.1 copy-done.8
  71.0 0.5 fusion.106
  71.6 41.0 %all-to-all-done = f32[8,4,7,36,128]{4,1,3,2,0:T(4,128)} async-done(((f32[8,4,7,36,128]{4,1,3,2,0:T(4,128)}), f32[8,4,7,36,128]{4,1,3,2,0:T(4,128)}, u32[]{:S(2)}, u32[]{:S(2)}) %all-to-all-start) | async-done | bytes 4128800 | tf_op jit(solution)/shard_map/all_to_all | solution.py:203
  112.6 2.2 %slice.954 = f32[4,8,6,36,128]{4,0,3,2,1:T(4,128)S(1)} slice(f32[4,8,7,36,128]{4,0,3,2,1:T(4,128)} %bitcast.13), slice={[0:4], [0:8], [0:6], [0:36], [0:128]} | slice | bytes 7077888 | tf_op jit(solution)/shard_map/slice | solution.py:207
  114.8 0.7 slice_bitcast_fusion
  115.5 0.3 pad_dynamic-slice_fusion.1
  115.9 0.6 multiply_add_fusion
  116.5 3.9 %subtract_multiply_fusion = f32[4,14,36,128]{3,0,2,1:T(4,128)S(1)} fusion(s32[]{:T(128)S(6)} %select_n.216, s32[]{:T(128)S(6)} %select_n.215, f32[4,22,36,128]{3,0,2,1:T(4,128)S(1)} %pad_dynamic-slice_fusion.1, s32[]{:T(128)S(6)} %select_n.213, s32[]{:T(128)S(6)} %select_n.212, s32[]{:T(128)S(6)} %select_n.211, s32[]{:T(128)S(6)} %select_n.209, ...), kind=kLoop, calls=%fused_computation.28 | loop fusion | flops 5160960 | bytes 6193196 | tf_op jit(solution)/shard_map/mul | solution.py:130
  120.4 3.1 %fusion.93 = f32[4,6,36,128]{3,0,2,1:T(4,128)} fusion(f32[4,6,18,128]{3,0,2,1:T(4,128)S(1)} %get-tuple-element.129, f32[4,6,18,128]{3,0,2,1:T(4,128)S(1)} %get-tuple-element.128, f32[4,14,36,128]{3,0,2,1:T(4,128)S(1)} %subtract_multiply_fusion, s32[]{:T(128)S(6)} %select_n.224, s32[]{:T(128)S(6)} %select_n.223, s32[]{:T(128)S(6)} %select_n.221, ...), kind=kLoop, calls=%fused_computation.192 | loop fusion | flops 2322432 | bytes 2805800 | tf_op jit(solution)/shard_map/mul | solution.py:254
  (59 shorter events, 1.4 us)
Async XLA Ops:
  2.4 0.8 copy-start.3
  5.3 29.4 %collective-permute-start.2 = (f32[4,7,18,128]{3,0,2,1:T(4,128)S(1)}, f32[4,7,18,128]{3,0,2,1:T(4,128)S(1)}, u32[]{:S(2)}, u32[]{:S(2)}) collective-permute-start(f32[4,7,18,128]{3,0,2,1:T(4,128)S(1)} %get-tuple-element.123), channel_id=1, source_target_pairs={{1,0},{2,1},{3,2},{4,3},{5,4},{6,5},{7,6},{8,7},{9,8},{10,9},{11,1... | collective-permute-start | bytes 774152 | tf_op jit(solution)/shard_map/ppermute | solution.py:26
  6.6 28.2 %collective-permute-start.3 = (f32[4,7,18,128]{3,0,2,1:T(4,128)S(1)}, f32[4,7,18,128]{3,0,2,1:T(4,128)S(1)}, u32[]{:S(2)}, u32[]{:S(2)}) collective-permute-start(f32[4,7,18,128]{3,0,2,1:T(4,128)S(1)} %get-tuple-element.123), channel_id=1, source_target_pairs={{2,0},{3,1},{4,2},{5,3},{6,4},{7,5},{8,6},{9,7},{10,8},{11,9},{12,... | collective-permute-start | bytes 774152 | tf_op jit(solution)/shard_map/ppermute | solution.py:26
  7.9 26.9 %collective-permute-start.1 = (f32[4,7,18,128]{3,0,2,1:T(4,128)S(1)}, f32[4,7,18,128]{3,0,2,1:T(4,128)S(1)}, u32[]{:S(2)}, u32[]{:S(2)}) collective-permute-start(f32[4,7,18,128]{3,0,2,1:T(4,128)S(1)} %get-tuple-element.122), channel_id=1, source_target_pairs={{0,2},{1,3},{2,4},{3,5},{4,6},{5,7},{6,8},{7,9},{8,10},{9,11},{10,... | collective-permute-start | bytes 774152 | tf_op jit(solution)/shard_map/ppermute | solution.py:26
  14.4 20.3 %collective-permute-start = (f32[4,7,18,128]{3,0,2,1:T(4,128)S(1)}, f32[4,7,18,128]{3,0,2,1:T(4,128)S(1)}, u32[]{:S(2)}, u32[]{:S(2)}) collective-permute-start(f32[4,7,18,128]{3,0,2,1:T(4,128)S(1)} %get-tuple-element.122), channel_id=1, source_target_pairs={{0,1},{1,2},{2,3},{3,4},{4,5},{5,6},{6,7},{7,8},{8,9},{9,10},{10,1... | collective-permute-start | bytes 774152 | tf_op jit(solution)/shard_map/ppermute | solution.py:26
  42.5 1.2 copy-start.1
  47.5 2.7 %copy-start = (f32[9,6,18,128]{3,0,2,1:T(8,128)}, f32[9,6,18,128]{3,0,2,1:T(8,128)S(1)}, u32[]{:S(2)}) copy-start(f32[9,6,18,128]{3,0,2,1:T(8,128)S(1)} %get-tuple-element.49) | copy-start | bytes 1492996
  47.5 2.6 %copy-start.4 = (f32[4,6,36,128]{3,0,2,1:T(4,128)S(1)}, f32[4,6,36,128]{3,0,2,1:T(4,128)}, u32[]{:S(2)}) copy-start(f32[4,6,36,128]{3,0,2,1:T(4,128)} %copy-done.3) | copy-start | bytes 1327108
  52.7 59.9 %all-to-all-start = ((f32[8,4,7,36,128]{4,1,3,2,0:T(4,128)}), f32[8,4,7,36,128]{4,1,3,2,0:T(4,128)}, u32[]{:S(2)}, u32[]{:S(2)}) async-start(f32[8,4,7,36,128]{4,1,3,2,0:T(4,128)} %stack.2), calls=%async_computation | async-start | bytes 8257536 | tf_op jit(solution)/shard_map/all_to_all | solution.py:203
  69.6 1.0 copy-start.2
  69.6 1.1 copy-start.5
  69.6 1.3 %copy-start.7 = (f32[5,6,18,127]{3,0,2,1:T(8,128)S(1)}, f32[5,6,18,127]{3,0,2,1:T(8,128)}, u32[]{:S(2)}) copy-start(f32[5,6,18,127]{3,0,2,1:T(8,128)} %get-tuple-element.102) | copy-start | bytes 822964
  69.7 1.4 %copy-start.8 = (f32[5,6,18,127]{3,0,2,1:T(8,128)S(1)}, f32[5,6,18,127]{3,0,2,1:T(8,128)}, u32[]{:S(2)}) copy-start(f32[5,6,18,127]{3,0,2,1:T(8,128)} %get-tuple-element.103) | copy-start | bytes 822964
  114.8 1.1 copy-start.9
  114.8 1.1 copy-start.10
  115.9 4.5 %copy-start.6 = (f32[4,6,36,128]{3,0,2,1:T(4,128)S(1)}, f32[4,6,36,128]{3,0,2,1:T(4,128)}, u32[]{:S(2)}) copy-start(f32[4,6,36,128]{3,0,2,1:T(4,128)} %param.13) | copy-start | bytes 1327108
